TPU v7x, 256 devices: a whole 4x4x8 slice. The times are simulated.
256 devices in a mesh: row: 16 (over z, core), col: 16 (over x, y).
Axes of the slice: x: 4, y: 4, z: 8, core: 2. Of those that a mesh axis runs over, the one named last changes fastest.
Arguments:
- site_tensor: bfloat16 [1024, 4, 1024], P('row', None, 'col'), may hold values from -180 to 180
- site_tangent: bfloat16 [1024, 4, 1024], P('row', None, 'col'), may hold values from -180 to 180
- left_env: bfloat16 [1024, 16384], P('row', 'col'), may hold values from -0.1875 to 0.375
- right_env: bfloat16 [1024, 16384], P('row', 'col'), may hold values from -0.046875 to 0.09375
- mpo: bfloat16 [16, 16, 4, 4], replicated, may hold values from -0.25 to 0.75
- dissipation: float32 [4], replicated, may hold values from 0.2 to 2
Outputs:
- evolved: float32 [1024, 4, 1024], P('row', None, 'col')
- evolved_tangent: float32 [1024, 4, 1024], P('row', None, 'col')
All inputs are finite; a program needn't handle non-finite values.
Results may differ from a plain program's by a relative error of at most 0.0055.
Values may be sent and summed in bfloat16 or wider, within the bound.
No kernel may reach another device: no remote copies, remote signals or barrier semaphores. Data moves between devices by JAX's collectives and lax.ppermute only.
A program may use at most 64 MiB of HBM per device.

v0:
```python
import jax
import jax.numpy as jnp
from jax import lax
from jax.sharding import PartitionSpec as P

KRYLOV = 3
taylor_order = 16


def inner(first, second):
    return jnp.sum(first * second)


def taylor(hess, dhess):
    size = hess.shape[0]
    term = jnp.zeros((size,), jnp.float32).at[0].set(1.0)
    dterm = jnp.zeros((size,), jnp.float32)
    total = term
    dtotal = dterm
    for order in range(1, taylor_order + 1):
        nterm = jnp.dot(hess, term, precision=lax.Precision.HIGHEST) / order
        dterm = (
            jnp.dot(dhess, term, precision=lax.Precision.HIGHEST)
            + jnp.dot(hess, dterm, precision=lax.Precision.HIGHEST)
        ) / order
        term = nterm
        total = total + term
        dtotal = dtotal + dterm
    return (total, dtotal)


def local(site_tensor, site_tangent, left_env, right_env, mpo, dissipation):
    rows_here, physical, cols_here = site_tensor.shape
    channels = mpo.shape[0]
    left_whole = lax.all_gather(left_env, "col", axis=1, tiled=True)
    right_whole = lax.all_gather(right_env, "row", axis=0, tiled=True)

    def apply(stacked):
        panels = stacked.shape[1]
        whole = lax.all_gather(stacked.astype(jnp.bfloat16), "row", axis=0, tiled=True)
        flat = whole.reshape(whole.shape[0], panels * physical * cols_here)
        left_three = left_whole.reshape(rows_here, flat.shape[0], channels)
        mixed = lax.dot_general(
            left_three, flat, (((1,), (0,)), ((), ())), preferred_element_type=jnp.float32
        )
        mixed = mixed.astype(jnp.bfloat16).reshape(rows_here, channels, panels, physical, cols_here)
        channel = jnp.einsum("awspr,wvpq->asqrv", mixed, mpo, preferred_element_type=jnp.float32)
        channel = channel.astype(jnp.bfloat16).reshape(
            rows_here * panels * physical, cols_here * channels
        )
        partial_rows = lax.dot_general(
            channel, right_whole, (((1,), (1,)), ((), ())), preferred_element_type=jnp.float32
        )
        partial_rows = partial_rows.reshape(rows_here, panels, physical, partial_rows.shape[1])
        summed = lax.psum_scatter(partial_rows, "col", scatter_dimension=3, tiled=True)
        return summed - dissipation[None, None, :, None] * stacked

    primal = site_tensor.astype(jnp.float32)
    tangent = site_tangent.astype(jnp.float32)
    starting = lax.psum(jnp.stack([inner(primal, primal), inner(primal, tangent)]), ("row", "col"))
    norm_site = jnp.sqrt(starting[0])
    norm_tangent = starting[1] / norm_site
    basis = [primal / norm_site]
    tangents = [(tangent - basis[0] * norm_tangent) / norm_site]
    hess = jnp.zeros((KRYLOV, KRYLOV), jnp.float32)
    dhess = jnp.zeros((KRYLOV, KRYLOV), jnp.float32)
    for level in range(KRYLOV):
        image = apply(basis[level][:, None])[:, 0]
        dimage = apply(tangents[level][:, None])[:, 0]
        counted = level + 1
        locals_list = [inner(vector, image) for vector in basis]
        locals_list = locals_list + [inner(vector, image) for vector in tangents]
        locals_list = locals_list + [inner(vector, dimage) for vector in basis]
        totals = lax.psum(jnp.stack(locals_list), ("row", "col"))
        coeffs = totals[:counted]
        across = totals[counted : 2 * counted]
        along = totals[2 * counted : 3 * counted]
        dcoeffs = across + along
        hess = hess.at[:counted, level].set(coeffs)
        dhess = dhess.at[:counted, level].set(dcoeffs)
        if level + 1 < KRYLOV:
            residual = image
            dresidual = dimage
            for index in range(counted):
                residual = residual - coeffs[index] * basis[index]
                dresidual = (
                    dresidual - dcoeffs[index] * basis[index] - coeffs[index] * tangents[index]
                )
            paired = lax.psum(
                jnp.stack([inner(residual, residual), inner(residual, dresidual)]), ("row", "col")
            )
            squared = paired[0]
            mixed_term = paired[1]
            height = jnp.sqrt(squared)
            dheight = mixed_term / height
            newvec = residual / height
            basis.append(newvec)
            tangents.append((dresidual - newvec * dheight) / height)
            hess = hess.at[level + 1, level].set(height)
            dhess = dhess.at[level + 1, level].set(dheight)
    coeff, dcoeff = taylor(hess, dhess)
    spread = jnp.zeros_like(primal)
    dspread = jnp.zeros_like(primal)
    for index in range(KRYLOV):
        spread = spread + coeff[index] * basis[index]
        dspread = dspread + coeff[index] * tangents[index] + dcoeff[index] * basis[index]
    evolved = norm_site * spread
    evolved_tangent = norm_tangent * spread + norm_site * dspread
    return (evolved, evolved_tangent)


def solution(mesh):
    in_specs = (
        P("row", None, "col"),
        P("row", None, "col"),
        P("row", "col"),
        P("row", "col"),
        P(),
        P(),
    )
    out_specs = (P("row", None, "col"), P("row", None, "col"))
    return jax.shard_map(local, mesh=mesh, in_specs=in_specs, out_specs=out_specs, check_vma=False)
```

profile of v0, /device:TPU:1, one launch (start us, length us, event | category | flops | bytes accessed | tf_op | source)
XLA Modules:
  0.0 1113.4 jit_solution(7619003044250572234)
XLA Ops:
  11.6 81.9 %psum.42 = f32[2]{0:T(128)S(1)} all-reduce(f32[2]{0:T(128)S(1)} %pad_maximum_fusion), channel_id=1, replica_groups=mesh['row'=16,'col'=16] {'row','col'}, use_global_device_ids=true, to_apply=%region_2.0 | all-reduce | flops 2 | bytes 16 | tf_op jit(solution)/shard_map/psum | solution.py:60
  96.4 18.8 %all-gather = bf16[1024,4,64]{2,1,0:T(4,128)(2,1)S(1)} all-gather(bf16[64,4,64]{2,1,0:T(4,128)(2,1)S(1)} %get-tuple-element.182), channel_id=2, replica_groups=mesh['row'=16,'col'=16] {'row'}, dimensions={0}, use_global_device_ids=true | all-gather | bytes 557056 | tf_op jit(solution)/shard_map/all_gather | solution.py:40
  116.0 4.8 copy.120
  120.8 4.5 copy.122
  137.6 18.6 %all-gather.1 = bf16[1024,4,64]{2,1,0:T(4,128)(2,1)S(1)} all-gather(bf16[64,4,64]{2,1,0:T(4,128)(2,1)S(1)} %get-tuple-element.181), channel_id=3, replica_groups=mesh['row'=16,'col'=16] {'row'}, dimensions={0}, use_global_device_ids=true | all-gather | bytes 557056 | tf_op jit(solution)/shard_map/all_gather | solution.py:40
  173.1 37.3 %reduce-scatter.19.cloned.1.call-done = f32[64,256]{1,0:T(8,128)} async-done(((f32[1024,256]{1,0:T(8,128)}), f32[64,256]{1,0:T(8,128)}) %reduce-scatter.19.cloned.1.call-update) | async-done | bytes 65552
  211.4 80.8 %reduce-scatter.21.cloned.1.call-done = f32[64,256]{1,0:T(8,128)} async-done(((f32[1024,256]{1,0:T(8,128)}), f32[64,256]{1,0:T(8,128)}) %reduce-scatter.21.cloned.1.call-update) | async-done | bytes 65552
  296.1 77.2 %psum.43 = f32[3]{0:T(128)S(1)} all-reduce(f32[3]{0:T(128)S(1)} %pad_maximum_fusion.1), channel_id=1, replica_groups=mesh['row'=16,'col'=16] {'row','col'}, use_global_device_ids=true, to_apply=%region_8.0 | all-reduce | flops 3 | bytes 24 | tf_op jit(solution)/shard_map/psum | solution.py:74
  378.1 73.2 %psum.44 = f32[2]{0:T(128)S(1)} all-reduce(f32[2]{0:T(128)S(1)} %pad_maximum_fusion.2), channel_id=1, replica_groups=mesh['row'=16,'col'=16] {'row','col'}, use_global_device_ids=true, to_apply=%region_11.0 | all-reduce | flops 2 | bytes 16 | tf_op jit(solution)/shard_map/psum | solution.py:89
  453.9 18.9 %all-gather.2 = bf16[1024,4,64]{2,1,0:T(4,128)(2,1)S(1)} all-gather(bf16[64,4,64]{2,1,0:T(4,128)(2,1)S(1)} %get-tuple-element.180), channel_id=4, replica_groups=mesh['row'=16,'col'=16] {'row'}, dimensions={0}, use_global_device_ids=true | all-gather | bytes 557056 | tf_op jit(solution)/shard_map/all_gather | solution.py:40
  493.5 18.4 %all-gather.3 = bf16[1024,4,64]{2,1,0:T(4,128)(2,1)S(1)} all-gather(bf16[64,4,64]{2,1,0:T(4,128)(2,1)} %get-tuple-element.173), channel_id=5, replica_groups=mesh['row'=16,'col'=16] {'row'}, dimensions={0}, use_global_device_ids=true | all-gather | bytes 557056 | tf_op jit(solution)/shard_map/all_gather | solution.py:40
  521.4 3.6 copy.149
  532.6 33.9 %reduce-scatter.23.cloned.1.call-done = f32[64,256]{1,0:T(8,128)} async-done(((f32[1024,256]{1,0:T(8,128)}), f32[64,256]{1,0:T(8,128)}) %reduce-scatter.23.cloned.1.call-update) | async-done | bytes 65552
  567.6 80.8 %reduce-scatter.25.cloned.1.call-done = f32[64,256]{1,0:T(8,128)} async-done(((f32[1024,256]{1,0:T(8,128)}), f32[64,256]{1,0:T(8,128)}) %reduce-scatter.25.cloned.1.call-update) | async-done | bytes 65552
  650.4 3.9 stack.106
  654.3 77.2 %psum.45 = f32[6]{0:T(128)S(1)} all-reduce(f32[6]{0:T(128)S(1)} %stack.106), channel_id=1, replica_groups=mesh['row'=16,'col'=16] {'row','col'}, use_global_device_ids=true, to_apply=%region_20.0 | all-reduce | flops 6 | bytes 48 | tf_op jit(solution)/shard_map/psum | solution.py:74
  737.5 73.3 %psum.46 = f32[2]{0:T(128)S(1)} all-reduce(f32[2]{0:T(128)S(1)} %pad_maximum_fusion.3), channel_id=1, replica_groups=mesh['row'=16,'col'=16] {'row','col'}, use_global_device_ids=true, to_apply=%region_23.0 | all-reduce | flops 2 | bytes 16 | tf_op jit(solution)/shard_map/psum | solution.py:89
  813.4 18.9 %all-gather.5 = bf16[1024,4,64]{2,1,0:T(4,128)(2,1)S(1)} all-gather(bf16[64,4,64]{2,1,0:T(4,128)(2,1)S(1)} %get-tuple-element.168), channel_id=7, replica_groups=mesh['row'=16,'col'=16] {'row'}, dimensions={0}, use_global_device_ids=true | all-gather | bytes 557056 | tf_op jit(solution)/shard_map/all_gather | solution.py:40
  853.1 18.5 %all-gather.4 = bf16[1024,4,64]{2,1,0:T(4,128)(2,1)S(1)} all-gather(bf16[64,4,64]{2,1,0:T(4,128)(2,1)} %get-tuple-element.179), channel_id=6, replica_groups=mesh['row'=16,'col'=16] {'row'}, dimensions={0}, use_global_device_ids=true | all-gather | bytes 557056 | tf_op jit(solution)/shard_map/all_gather | solution.py:40
  894.8 31.1 %reduce-scatter.29.cloned.1.call-done = f32[64,256]{1,0:T(8,128)} async-done(((f32[1024,256]{1,0:T(8,128)}), f32[64,256]{1,0:T(8,128)}) %reduce-scatter.29.cloned.1.call-update) | async-done | bytes 65552
  927.0 80.9 %reduce-scatter.27.cloned.1.call-done = f32[64,256]{1,0:T(8,128)} async-done(((f32[1024,256]{1,0:T(8,128)}), f32[64,256]{1,0:T(8,128)}) %reduce-scatter.27.cloned.1.call-update) | async-done | bytes 65552
  1010.3 5.8 stack.119
  1016.2 77.2 %psum.47 = f32[9]{0:T(128)S(1)} all-reduce(f32[9]{0:T(128)S(1)} %stack.119), channel_id=1, replica_groups=mesh['row'=16,'col'=16] {'row','col'}, use_global_device_ids=true, to_apply=%region_35.0 | all-reduce | flops 9 | bytes 72 | tf_op jit(solution)/shard_map/psum | solution.py:74
  1101.5 4.5 multiply_add_fusion
  (187 shorter events, 149.0 us)
Async XLA Ops:
  7.2 108.7 %copy-start.8 = (bf16[16,16,4,4]{1,3,2,0:T(4,128)(2,1)S(1)}, bf16[16,16,4,4]{1,3,2,0:T(4,128)(2,1)}, u32[]{:S(2)}) copy-start(bf16[16,16,4,4]{1,3,2,0:T(4,128)(2,1)} %param.32) | copy-start | bytes 24580
  7.2 108.9 %all-gather.9.cloned.1.call-start = ((), (), s32[]{:S(2)}) async-start(), calls=%async_computation.6 | async-start | bytes 2228224 | tf_op jit(solution)/shard_map/all_gather | solution.py:35
  7.9 123.7 %all-gather.11.cloned.1.call-start = ((), (), s32[]{:S(2)}) async-start(), calls=%async_computation.7 | async-start | bytes 2228224 | tf_op jit(solution)/shard_map/all_gather | solution.py:36
  8.7 201.7 %reduce-scatter.19.cloned.1.call-start = ((), (), s32[]{:S(2)}) async-start(), calls=%async_computation.8 | async-start | bytes 1114112
  116.0 43.8 %copy-start.9 = (bf16[16,16,4,4]{0,1,2,3:T(8,128)(2,1)}, bf16[16,16,4,4]{0,1,2,3:T(8,128)(2,1)S(1)}, u32[]{:S(2)}) copy-start(bf16[16,16,4,4]{0,1,2,3:T(8,128)(2,1)S(1)} %copy.124) | copy-start | bytes 24580
  125.3 3.6 copy-start.5
  137.6 20.1 %copy-start.6 = (bf16[64,1024,16]{1,0,2:T(8,128)(2,1)S(1)}, bf16[64,1024,16]{1,0,2:T(8,128)(2,1)}, u32[]{:S(2)}) copy-start(bf16[64,1024,16]{1,0,2:T(8,128)(2,1)} %copy-done.5) | copy-start | bytes 6291460
  137.6 154.6 %reduce-scatter.21.cloned.1.call-start = ((), (), s32[]{:S(2)}) async-start(), calls=%async_computation.9 | async-start | bytes 1114112
  159.9 5.6 copy-start
  169.7 123.6 %copy-start.1 = (bf16[64,4,64]{2,1,0:T(4,128)(2,1)S(1)}, bf16[64,4,64]{2,1,0:T(4,128)(2,1)}, u32[]{:S(2)}) copy-start(bf16[64,4,64]{2,1,0:T(4,128)(2,1)} %param.28) | copy-start | bytes 98308
  169.7 123.6 %copy-start.2 = (bf16[64,4,64]{2,1,0:T(4,128)(2,1)S(1)}, bf16[64,4,64]{2,1,0:T(4,128)(2,1)}, u32[]{:S(2)}) copy-start(bf16[64,4,64]{2,1,0:T(4,128)(2,1)} %param.29) | copy-start | bytes 98308
  169.7 123.6 %copy-start.10 = (f32[4]{0:T(128)S(1)}, f32[4]{0:T(128)}, u32[]{:S(2)}) copy-start(f32[4]{0:T(128)} %param.33) | copy-start | bytes 52
  173.0 393.5 %reduce-scatter.23.cloned.1.call-start = ((), (), s32[]{:S(2)}) async-start(), calls=%async_computation.10 | async-start | bytes 1114112
  493.4 154.9 %reduce-scatter.25.cloned.1.call-start = ((), (), s32[]{:S(2)}) async-start(), calls=%async_computation.11 | async-start | bytes 1114112
  532.6 393.4 %reduce-scatter.29.cloned.1.call-start = ((), (), s32[]{:S(2)}) async-start(), calls=%async_computation.13 | async-start | bytes 1114112
  736.2 77.2 %copy-start.3 = (f32[64,4,64]{2,1,0:T(4,128)}, f32[64,4,64]{2,1,0:T(4,128)S(1)}, u32[]{:S(2)}) copy-start(f32[64,4,64]{2,1,0:T(4,128)S(1)} %get-tuple-element.171) | copy-start | bytes 196612
  853.0 155.0 %reduce-scatter.27.cloned.1.call-start = ((), (), s32[]{:S(2)}) async-start(), calls=%async_computation.12 | async-start | bytes 1114112
  888.2 120.9 %copy-start.4 = (f32[64,4,64]{2,1,0:T(4,128)S(1)}, f32[64,4,64]{2,1,0:T(4,128)}, u32[]{:S(2)}) copy-start(f32[64,4,64]{2,1,0:T(4,128)} %copy-done.3) | copy-start | bytes 196612
  888.2 120.9 %copy-start.7 = (f32[64,4,64]{2,1,0:T(4,128)S(1)}, f32[64,4,64]{2,1,0:T(4,128)}, u32[]{:S(2)}) copy-start(f32[64,4,64]{2,1,0:T(4,128)} %get-tuple-element.169) | copy-start | bytes 196612
  890.3 203.3 %copy-start.11 = (f32[3,1]{0,1:T(1,128)S(1)}, f32[3,1]{0,1:T(1,128)}, u32[]{:S(2)}) copy-start(f32[3,1]{0,1:T(1,128)} %constant.327) | copy-start | bytes 40
Sparse Core Ops, SparseCore 0:
  10.5 52.1 all-gather.8
  64.5 40.9 all-gather.10
  137.7 72.6 reduce-scatter.18
  213.7 78.4 reduce-scatter.20
  493.6 72.8 reduce-scatter.22
  569.8 78.4 reduce-scatter.24
  853.1 72.8 reduce-scatter.28
  929.5 78.4 reduce-scatter.26
where the time goes:
time: 1120 us; the launch traced here: 1110 us
  blocking collectives  572 us (51%)
  waiting for transfers between devices  346 us (31%)
  local copies, waits for them, and re-layouts  98.9 us (9%)
  matrix products  52.6 us (5%)
  other arithmetic  22.7 us (2%)
  between operations  20.4 us (2%)
    unnamed x14, waiting for transfers between devices  346 us
    psum x3, blocking collectives, local(): totals = lax.psum(jnp.stack(locals_list), ('row', 'col'))  232 us
    psum x2, blocking collectives, local(): lax.psum(jnp.stack([inner(residual, residual), inner(residual, dresidual)...  146 us
    all_gather x6, blocking collectives, apply(): lax.all_gather(stacked.astype(jnp.bfloat16), 'row', axis=0, tiled=True)  112 us
    psum x1, blocking collectives, local(): lax.psum(jnp.stack([inner(primal, primal), inner(primal, tangent)]), ('ro...  81.9 us
    unnamed x43, local copies, waits for them, and re-layouts  31.9 us
  transfers between devices with their start and end apart: 8, of which 6 were waited for; matrix products, arithmetic and copies ran while one was open for 8% of the time, Pallas kernels for 0%

commit v1 on v0

--- a/solution.py
+++ b/solution.py
@@ -37,7 +37,25 @@
 
     def apply(stacked):
         panels = stacked.shape[1]
-        whole = lax.all_gather(stacked.astype(jnp.bfloat16), "row", axis=0, tiled=True)
+        x = stacked.astype(jnp.bfloat16)
+        length, index_2, extent = (lax.axis_size("row"), lax.axis_index("row"), x.shape[0])
+        right = [(i, (i + 1) % length) for i in range(length)]
+        backward = [(i, (i - 1) % length) for i in range(length)]
+        filled = jnp.zeros((*x.shape[:0], length * extent, *x.shape[0 + 1 :]), x.dtype)
+        filled = lax.dynamic_update_slice_in_dim(filled, x, index_2 * extent, axis=0)
+        from_left = from_right = x
+        half = length // 2
+        for step in range(1, half + 1):
+            from_left = lax.ppermute(from_left, "row", right)
+            filled = lax.dynamic_update_slice_in_dim(
+                filled, from_left, (index_2 - step) % length * extent, axis=0
+            )
+            if step < length - half:
+                from_right = lax.ppermute(from_right, "row", backward)
+                filled = lax.dynamic_update_slice_in_dim(
+                    filled, from_right, (index_2 + step) % length * extent, axis=0
+                )
+        whole = filled
         flat = whole.reshape(whole.shape[0], panels * physical * cols_here)
         left_three = left_whole.reshape(rows_here, flat.shape[0], channels)
         mixed = lax.dot_general(

time: 1120 us -> 1220 us (1.089)
  starting transfers between devices: 0.32 us -> 159 us
  blocking collectives: 572 us -> 460 us
  local copies, waits for them, and re-layouts: 98.9 us -> 199 us
  waiting for transfers between devices: 346 us -> 293 us
    ppermute x0 -> x90, starting transfers between devices: none -> 159 us  [the longest x42 137 us: apply(): from_right = lax.ppermute(from_right, 'row', backward)]
    all_gather x6 -> x0, blocking collectives: 112 us -> none  [apply(): lax.all_gather(stacked.astype(jnp.bfloat16), 'row', axis=0, tiled=True)]
    dynamic_update_slice x0 -> x96, local copies, waits for them, and re-layouts: none -> 91.9 us  [the longest x48 46 us: apply(): lax.dynamic_update_slice_in_dim(filled, from_left, (index_2 - step) % len...]
    unnamed x14, waiting for transfers between devices: 346 us -> 256 us
    ppermute x0 -> x90, waiting for transfers between devices: none -> 37.5 us  [the longest x48 30.7 us: apply(): from_left = lax.ppermute(from_left, 'row', right)]
    unnamed x43 -> x85, local copies, waits for them, and re-layouts: 31.9 us -> 47.5 us
  transfers between devices with their start and end apart: 8 -> 98, of which waited for: 6 -> 74; matrix products, arithmetic and copies ran while one was open for 8% -> 15% of each run, Pallas kernels for 0% -> 0%
where the time goes in v1:
time: 1220 us; the launch traced here: 1200 us
  blocking collectives  460 us (38%)
  waiting for transfers between devices  293 us (24%)
  local copies, waits for them, and re-layouts  199 us (16%)
  starting transfers between devices  159 us (13%)
  matrix products  50.3 us (4%)
  between operations  21.5 us (2%)
  other arithmetic  19.3 us (2%)
    unnamed x14, waiting for transfers between devices  256 us
    psum x3, blocking collectives, local(): totals = lax.psum(jnp.stack(locals_list), ('row', 'col'))  232 us
    psum x2, blocking collectives, local(): lax.psum(jnp.stack([inner(residual, residual), inner(residual, dresidual)...  146 us
    ppermute x42, starting transfers between devices, apply(): from_right = lax.ppermute(from_right, 'row', backward)  137 us
    psum x1, blocking collectives, local(): lax.psum(jnp.stack([inner(primal, primal), inner(primal, tangent)]), ('ro...  81.7 us
    unnamed x85, local copies, waits for them, and re-layouts  47.5 us
    dynamic_update_slice x48, local copies, waits for them, and re-layouts, apply(): lax.dynamic_update_slice_in_dim(filled, from_left, (index_2 - step) % len...  46 us
    dynamic_update_slice x42, local copies, waits for them, and re-layouts, apply(): lax.dynamic_update_slice_in_dim(filled, from_right, (index_2 + step) % le...  39.9 us
  transfers between devices with their start and end apart: 98, of which 74 were waited for; matrix products, arithmetic and copies ran while one was open for 15% of the time, Pallas kernels for 0%

profile of v1, /device:TPU:1, one launch (start us, length us, event | category | flops | bytes accessed | tf_op | source)
XLA Modules:
  0.0 1202.3 jit_solution(14216410660020975127)
XLA Ops:
  12.6 81.7 %psum.42 = f32[2]{0:T(128)S(1)} all-reduce(f32[2]{0:T(128)S(1)} %pad_maximum_fusion), channel_id=1, replica_groups=mesh['row'=16,'col'=16] {'row','col'}, use_global_device_ids=true, to_apply=%region_2.0 | all-reduce | flops 2 | bytes 16 | tf_op jit(solution)/shard_map/psum | solution.py:78
  139.4 4.8 copy.259
  144.2 4.5 copy.261
  161.2 4.2 collective-permute-start.1
  223.5 13.1 %reshape.589 = f32[1024,256]{1,0:T(8,128)} reshape(f32[1024,1,4,64]{3,2,1,0:T(4,128)} %bitcast.725) | data formatting | bytes 2097152
  238.3 80.9 %reduce-scatter.19.cloned.1.call-done = f32[64,256]{1,0:T(8,128)} async-done(((f32[1024,256]{1,0:T(8,128)}), f32[64,256]{1,0:T(8,128)}) %reduce-scatter.19.cloned.1.call-update) | async-done | bytes 65552
  322.8 77.2 %psum.43 = f32[3]{0:T(128)S(1)} all-reduce(f32[3]{0:T(128)S(1)} %pad_maximum_fusion.1), channel_id=1, replica_groups=mesh['row'=16,'col'=16] {'row','col'}, use_global_device_ids=true, to_apply=%region_8.9 | all-reduce | flops 3 | bytes 24 | tf_op jit(solution)/shard_map/psum | solution.py:92
  404.6 73.3 %psum.44 = f32[2]{0:T(128)S(1)} all-reduce(f32[2]{0:T(128)S(1)} %pad_maximum_fusion.2), channel_id=1, replica_groups=mesh['row'=16,'col'=16] {'row','col'}, use_global_device_ids=true, to_apply=%region_11.12 | all-reduce | flops 2 | bytes 16 | tf_op jit(solution)/shard_map/psum | solution.py:107
  496.8 4.0 collective-permute-start.39
  501.7 4.0 collective-permute-start.41
  547.8 4.1 collective-permute-start.46
  567.5 4.0 collective-permute-start.54
  572.4 4.2 collective-permute-start.56
  618.1 6.8 reduce-scatter.23.cloned.1.call-done
  625.8 80.8 %reduce-scatter.25.cloned.1.call-done = f32[64,256]{1,0:T(8,128)} async-done(((f32[1024,256]{1,0:T(8,128)}), f32[64,256]{1,0:T(8,128)}) %reduce-scatter.25.cloned.1.call-update) | async-done | bytes 65552
  712.4 77.2 %psum.45 = f32[6]{0:T(128)S(1)} all-reduce(f32[6]{0:T(128)S(1)} %stack.106), channel_id=1, replica_groups=mesh['row'=16,'col'=16] {'row','col'}, use_global_device_ids=true, to_apply=%region_20.21 | all-reduce | flops 6 | bytes 48 | tf_op jit(solution)/shard_map/psum | solution.py:92
  795.4 73.2 %psum.46 = f32[2]{0:T(128)S(1)} all-reduce(f32[2]{0:T(128)S(1)} %pad_maximum_fusion.3), channel_id=1, replica_groups=mesh['row'=16,'col'=16] {'row','col'}, use_global_device_ids=true, to_apply=%region_23.24 | all-reduce | flops 2 | bytes 16 | tf_op jit(solution)/shard_map/psum | solution.py:107
  937.6 4.1 collective-permute-start.61
  957.3 4.0 collective-permute-start.69
  962.3 4.2 collective-permute-start.71
  1010.7 4.1 reduce-scatter.29.cloned.1.call-done
  1015.7 81.0 %reduce-scatter.27.cloned.1.call-done = f32[64,256]{1,0:T(8,128)} async-done(((f32[1024,256]{1,0:T(8,128)}), f32[64,256]{1,0:T(8,128)}) %reduce-scatter.27.cloned.1.call-update) | async-done | bytes 65552
  1098.6 5.7 stack.119
  1104.5 77.2 %psum.47 = f32[9]{0:T(128)S(1)} all-reduce(f32[9]{0:T(128)S(1)} %stack.119), channel_id=1, replica_groups=mesh['row'=16,'col'=16] {'row','col'}, use_global_device_ids=true, to_apply=%region_35.36 | all-reduce | flops 9 | bytes 72 | tf_op jit(solution)/shard_map/psum | solution.py:92
  (493 shorter events, 402.5 us)
Async XLA Ops:
  7.2 132.2 %all-gather.3.cloned.1.call-start = ((), (), s32[]{:S(2)}) async-start(), calls=%async_computation.6 | async-start | bytes 2228224 | tf_op jit(solution)/shard_map/all_gather | solution.py:35
  7.9 147.3 %all-gather.5.cloned.1.call-start = ((), (), s32[]{:S(2)}) async-start(), calls=%async_computation.7 | async-start | bytes 2228224 | tf_op jit(solution)/shard_map/all_gather | solution.py:36
  8.6 228.7 %reduce-scatter.21.cloned.1.call-start = ((), (), s32[]{:S(2)}) async-start(), calls=%async_computation.9 | async-start | bytes 1114112
  123.3 14.7 %collective-permute-start.28 = (bf16[64,1,4,64]{0,3,2,1:T(8,128)(2,1)S(1)}, bf16[64,1,4,64]{0,3,2,1:T(8,128)(2,1)S(1)}, u32[]{:S(2)}, u32[]{:S(2)}) collective-permute-start(bf16[64,1,4,64]{0,3,2,1:T(8,128)(2,1)S(1)} %collective-permute-done.26), channel_id=1, source_target_pairs={{0,240},{16,0},{32,16},{48,32},{64,48},{80,64},{96,80},{112,96},{1... | collective-permute-start | bytes 98312 | tf_op jit(solution)/shard_map/ppermute | solution.py:54
  127.6 10.8 collective-permute-start.29
  161.1 158.0 %reduce-scatter.19.cloned.1.call-start = ((), (), s32[]{:S(2)}) async-start(), calls=%async_computation.8 | async-start | bytes 1114112
  161.2 5.1 collective-permute-start.1
  190.9 16.3 %collective-permute-start.13 = (bf16[64,1,4,64]{0,3,2,1:T(8,128)(2,1)}, bf16[64,1,4,64]{0,3,2,1:T(8,128)(2,1)}, u32[]{:S(2)}, u32[]{:S(2)}) collective-permute-start(bf16[64,1,4,64]{0,3,2,1:T(8,128)(2,1)} %collective-permute-done.11), channel_id=1, source_target_pairs={{0,240},{16,0},{32,16},{48,32},{64,48},{80,64},{96,80},{112,96},{1... | collective-permute-start | bytes 98312 | tf_op jit(solution)/shard_map/ppermute | solution.py:54
  195.7 12.7 %collective-permute-start.14 = (bf16[64,1,4,64]{0,3,2,1:T(8,128)(2,1)}, bf16[64,1,4,64]{0,3,2,1:T(8,128)(2,1)}, u32[]{:S(2)}, u32[]{:S(2)}) collective-permute-start(bf16[64,1,4,64]{0,3,2,1:T(8,128)(2,1)} %collective-permute-done.12), channel_id=1, source_target_pairs={{0,16},{16,32},{32,48},{48,64},{64,80},{80,96},{96,112},{112,128},... | collective-permute-start | bytes 98312 | tf_op jit(solution)/shard_map/ppermute | solution.py:49
  236.6 388.3 %reduce-scatter.23.cloned.1.call-start = ((), (), s32[]{:S(2)}) async-start(), calls=%async_computation.10 | async-start | bytes 1114112
  506.8 18.6 %collective-permute-start.43 = (bf16[64,1,4,64]{0,3,2,1:T(8,128)(2,1)}, bf16[64,1,4,64]{0,3,2,1:T(8,128)(2,1)}, u32[]{:S(2)}, u32[]{:S(2)}) collective-permute-start(bf16[64,1,4,64]{0,3,2,1:T(8,128)(2,1)} %collective-permute-done.41), channel_id=1, source_target_pairs={{0,240},{16,0},{32,16},{48,32},{64,48},{80,64},{96,80},{112,96},{1... | collective-permute-start | bytes 98312 | tf_op jit(solution)/shard_map/ppermute | solution.py:54
  511.5 14.9 %collective-permute-start.44 = (bf16[64,1,4,64]{0,3,2,1:T(8,128)(2,1)}, bf16[64,1,4,64]{0,3,2,1:T(8,128)(2,1)}, u32[]{:S(2)}, u32[]{:S(2)}) collective-permute-start(bf16[64,1,4,64]{0,3,2,1:T(8,128)(2,1)} %collective-permute-done.42), channel_id=1, source_target_pairs={{0,16},{16,32},{32,48},{48,64},{64,80},{80,96},{96,112},{112,128},... | collective-permute-start | bytes 98312 | tf_op jit(solution)/shard_map/ppermute | solution.py:49
  547.7 159.0 %reduce-scatter.25.cloned.1.call-start = ((), (), s32[]{:S(2)}) async-start(), calls=%async_computation.11 | async-start | bytes 1114112
  572.4 5.2 collective-permute-start.56
  577.6 18.4 %collective-permute-start.58 = (bf16[64,1,4,64]{0,3,2,1:T(8,128)(2,1)}, bf16[64,1,4,64]{0,3,2,1:T(8,128)(2,1)}, u32[]{:S(2)}, u32[]{:S(2)}) collective-permute-start(bf16[64,1,4,64]{0,3,2,1:T(8,128)(2,1)} %collective-permute-done.56), channel_id=1, source_target_pairs={{0,240},{16,0},{32,16},{48,32},{64,48},{80,64},{96,80},{112,96},{1... | collective-permute-start | bytes 98312 | tf_op jit(solution)/shard_map/ppermute | solution.py:54
  582.2 14.9 %collective-permute-start.59 = (bf16[64,1,4,64]{0,3,2,1:T(8,128)(2,1)}, bf16[64,1,4,64]{0,3,2,1:T(8,128)(2,1)}, u32[]{:S(2)}, u32[]{:S(2)}) collective-permute-start(bf16[64,1,4,64]{0,3,2,1:T(8,128)(2,1)} %collective-permute-done.57), channel_id=1, source_target_pairs={{0,16},{16,32},{32,48},{48,64},{64,80},{80,96},{96,112},{112,128},... | collective-permute-start | bytes 98312 | tf_op jit(solution)/shard_map/ppermute | solution.py:49
  618.1 396.7 %reduce-scatter.29.cloned.1.call-start = ((), (), s32[]{:S(2)}) async-start(), calls=%async_computation.13 | async-start | bytes 1114112
  897.5 20.1 %collective-permute-start.88 = (bf16[64,1,4,64]{0,3,2,1:T(8,128)(2,1)}, bf16[64,1,4,64]{0,3,2,1:T(8,128)(2,1)}, u32[]{:S(2)}, u32[]{:S(2)}) collective-permute-start(bf16[64,1,4,64]{0,3,2,1:T(8,128)(2,1)} %collective-permute-done.86), channel_id=1, source_target_pairs={{0,240},{16,0},{32,16},{48,32},{64,48},{80,64},{96,80},{112,96},{1... | collective-permute-start | bytes 98312 | tf_op jit(solution)/shard_map/ppermute | solution.py:54
  902.3 16.4 %collective-permute-start.89 = (bf16[64,1,4,64]{0,3,2,1:T(8,128)(2,1)}, bf16[64,1,4,64]{0,3,2,1:T(8,128)(2,1)}, u32[]{:S(2)}, u32[]{:S(2)}) collective-permute-start(bf16[64,1,4,64]{0,3,2,1:T(8,128)(2,1)} %collective-permute-done.87), channel_id=1, source_target_pairs={{0,16},{16,32},{32,48},{48,64},{64,80},{80,96},{96,112},{112,128},... | collective-permute-start | bytes 98312 | tf_op jit(solution)/shard_map/ppermute | solution.py:49
  937.5 159.2 %reduce-scatter.27.cloned.1.call-start = ((), (), s32[]{:S(2)}) async-start(), calls=%async_computation.12 | async-start | bytes 1114112
  937.6 5.0 collective-permute-start.61
  962.3 5.2 collective-permute-start.71
  967.5 18.4 %collective-permute-start.73 = (bf16[64,1,4,64]{0,3,2,1:T(8,128)(2,1)}, bf16[64,1,4,64]{0,3,2,1:T(8,128)(2,1)}, u32[]{:S(2)}, u32[]{:S(2)}) collective-permute-start(bf16[64,1,4,64]{0,3,2,1:T(8,128)(2,1)} %collective-permute-done.71), channel_id=1, source_target_pairs={{0,240},{16,0},{32,16},{48,32},{64,48},{80,64},{96,80},{112,96},{1... | collective-permute-start | bytes 98312 | tf_op jit(solution)/shard_map/ppermute | solution.py:54
  972.0 14.9 %collective-permute-start.74 = (bf16[64,1,4,64]{0,3,2,1:T(8,128)(2,1)}, bf16[64,1,4,64]{0,3,2,1:T(8,128)(2,1)}, u32[]{:S(2)}, u32[]{:S(2)}) collective-permute-start(bf16[64,1,4,64]{0,3,2,1:T(8,128)(2,1)} %collective-permute-done.72), channel_id=1, source_target_pairs={{0,16},{16,32},{32,48},{48,64},{64,80},{80,96},{96,112},{112,128},... | collective-permute-start | bytes 98312 | tf_op jit(solution)/shard_map/ppermute | solution.py:49
  (105 other events, 1277.4 us)
Sparse Core Ops, SparseCore 0:
  10.5 52.2 all-gather.2
  64.5 40.7 all-gather.4
  161.3 75.9 reduce-scatter.20
  240.7 78.4 reduce-scatter.18
  547.8 77.0 reduce-scatter.22
  628.2 78.3 reduce-scatter.24
  937.7 77.0 reduce-scatter.28
  1018.3 78.3 reduce-scatter.26
